TPU v7x, 32 devices: a whole 2x2x4 slice. The times are simulated.
32 devices in a mesh: row: 8 (over z, y), col: 4 (over x, core).
Axes of the slice: x: 2, y: 2, z: 4, core: 2. Of those that a mesh axis runs over, the one named last changes fastest.
Arguments:
- x_t: bfloat16 [128, 8192], P('col', 'row'), may hold values from -6 to 6
- tiles: bfloat16 [64, 128, 128], P('row'), may hold values from -0.375 to 0.375
- tile_owner: int32 [64, 1], P('row'), may hold values from 0 to 7; in each aligned block of 8 rows (0 to 7, 8 to 15, ...) at most 2 rows name the same one
- tile_local: int32 [64, 2], P('row'), may hold values from 0 to 7
- weight: bfloat16 [128, 256], replicated, may hold values from -0.5 to 0.5
- cotangent: bfloat16 [8192, 256], P('row'), may hold values from -0.0625 to 0.0625
Outputs:
- act: bfloat16 [8192, 256], P('row')
- grad_w: float32 [128, 256], P('col')
Inputs may be any that keep to these rules, and one draw needn't show every extreme that they name: `tile_owner`: within the 8 stored tiles of one index of row (aligned blocks of 8 rows) no owner appears more than 2 times, and some owner appears exactly 2 times.
All inputs are finite; a program needn't handle non-finite values.
Results may differ from a plain program's by a relative error of at most 0.0059.
Values may be sent and summed in bfloat16 or wider, within the bound.
No kernel may reach another device: no remote copies, remote signals or barrier semaphores. Data moves between devices by JAX's collectives and lax.ppermute only.
A program may use at most 64 MiB of HBM per device.

v0:
```python
import jax
import jax.numpy as jnp
from jax import lax
from jax.sharding import PartitionSpec as P


def body(x_t, tiles, tile_owner, tile_local, weight, cotangent):
    n_row = lax.axis_size("row")
    n_tiles, tile_dim = (tiles.shape[0], tiles.shape[1])
    feat_q, rows = x_t.shape
    n_blocks = rows // tile_dim
    capacity = 2 * (n_tiles // n_row)
    xb = x_t.reshape(feat_q, n_blocks, tile_dim).transpose(1, 0, 2)
    flat_blocks = xb.reshape(n_blocks, feat_q * tile_dim)
    owner = tile_owner[:, 0]
    row_local = tile_local[:, 0]
    col_local = tile_local[:, 1]
    owner_hot = (owner[:, None] == jnp.arange(n_row, dtype=jnp.int32)[None, :]).astype(jnp.int32)
    rank = jnp.sum(owner_hot * (jnp.cumsum(owner_hot, axis=0) - 1), axis=1)
    slot = owner * capacity + rank
    requests = (
        jnp.zeros((n_row * capacity,), jnp.int32).at[slot].set(col_local).reshape(n_row, capacity)
    )
    own_blocks = jnp.take(xb, row_local, axis=0)
    mirror_terms = jnp.einsum(
        "tfi,tij->tfj", own_blocks, tiles, preferred_element_type=jnp.float32
    ).astype(jnp.bfloat16)
    outgoing = jnp.zeros((n_row * capacity, feat_q * tile_dim), jnp.bfloat16)
    outgoing = (
        outgoing.at[slot]
        .set(mirror_terms.reshape(n_tiles, feat_q * tile_dim))
        .reshape(n_row, capacity, feat_q * tile_dim)
    )
    block_ids = lax.all_to_all(requests, "row", split_axis=0, concat_axis=0, tiled=True)
    picked = jnp.take(flat_blocks, block_ids, axis=0)
    fetched = lax.all_to_all(picked, "row", split_axis=0, concat_axis=0, tiled=True)
    incoming = lax.all_to_all(outgoing, "row", split_axis=0, concat_axis=0, tiled=True)
    fetched_tiles = jnp.take(fetched.reshape(n_row * capacity, feat_q, tile_dim), slot, axis=0)
    forward_terms = jnp.einsum(
        "tfj,tij->tfi", fetched_tiles, tiles, preferred_element_type=jnp.float32
    )
    block_range = jnp.arange(n_blocks, dtype=jnp.int32)
    row_hot = (row_local[:, None] == block_range[None, :]).astype(jnp.float32)
    local_sum = jnp.einsum("tfi,tb->fbi", forward_terms, row_hot, precision=lax.Precision.HIGHEST)
    in_hot = (block_ids.reshape(-1)[:, None] == block_range[None, :]).astype(jnp.bfloat16)
    mirror_sum = jnp.einsum(
        "sk,sb->bk",
        incoming.reshape(n_row * capacity, feat_q * tile_dim),
        in_hot,
        preferred_element_type=jnp.float32,
    )
    mirror_sum = mirror_sum.reshape(n_blocks, feat_q, tile_dim).transpose(1, 0, 2)
    z_part = (local_sum + mirror_sum).reshape(feat_q, rows).astype(jnp.bfloat16)
    w_rows = lax.dynamic_slice_in_dim(weight, lax.axis_index("col") * feat_q, feat_q, 0)
    partial_y = lax.dot_general(
        z_part, w_rows, (((0,), (0,)), ((), ())), preferred_element_type=jnp.float32
    )
    y_full = lax.psum(partial_y, "col")
    act = jax.nn.silu(y_full).astype(jnp.bfloat16)
    sig = jax.nn.sigmoid(y_full)
    grad_y = (cotangent.astype(jnp.float32) * sig * (1.0 + y_full * (1.0 - sig))).astype(
        jnp.bfloat16
    )
    grad_part = jnp.dot(z_part, grad_y, preferred_element_type=jnp.float32)
    grad_w = lax.psum(grad_part, "row")
    return (act, grad_w)


def solution(mesh):
    in_specs = (
        P("col", "row"),
        P("row", None, None),
        P("row", None),
        P("row", None),
        P(),
        P("row", None),
    )
    out_specs = (P("row", None), P("col", None))
    return jax.shard_map(body, mesh=mesh, in_specs=in_specs, out_specs=out_specs, check_vma=False)
```

profile of v0, /device:TPU:0, one launch (start us, length us, event | category | flops | bytes accessed | tf_op | source)
XLA Modules:
  0.0 130.2 jit_solution(15986856091040692897)
XLA Ops:
  7.2 0.0 copy-start
  7.2 0.8 fusion.37
  7.9 0.0 copy-start.2
  7.9 0.7 copy-done.2
  8.6 0.1 fusion.24
  8.7 0.2 select_reduce_fusion
  8.9 0.6 scatter_custom_fusion
  9.5 0.7 all_to_all.16
  10.2 0.0 copy-start.3
  10.2 7.4 %all-to-all-start = ((s32[8,1,2]{2,1,0:T(1,128)}), s32[8,1,2]{2,1,0:T(1,128)S(1)}, u32[]{:S(2)}, u32[]{:S(2)}) async-start(s32[8,1,2]{2,1,0:T(1,128)} %bitcast.7), calls=%async_computation | async-start | bytes 8192 | tf_op jit(solution)/shard_map/all_to_all | solution.py:34
  17.6 0.0 copy-done.3
  17.6 0.9 bitcast_bitcast_fusion.1
  18.5 0.6 gather_fusion.2
  19.0 0.0 copy-done
  19.1 0.2 fusion.1
  19.3 0.8 scatter_custom_fusion.1
  20.1 0.7 reshape.80
  20.8 3.1 %all-to-all-done = s32[8,1,2]{2,1,0:T(1,128)S(1)} async-done(((s32[8,1,2]{2,1,0:T(1,128)}), s32[8,1,2]{2,1,0:T(1,128)S(1)}, u32[]{:S(2)}, u32[]{:S(2)}) %all-to-all-start) | async-done | bytes 96 | tf_op jit(solution)/shard_map/all_to_all | solution.py:34
  24.0 3.4 %all-to-all-start.2 = ((bf16[8,2,4096]{2,1,0:T(2,128)(2,1)}), bf16[8,2,4096]{2,1,0:T(2,128)(2,1)S(1)}, u32[]{:S(2)}, u32[]{:S(2)}) async-start(bf16[8,2,4096]{2,1,0:T(2,128)(2,1)} %reshape.80), calls=%async_computation.2 | async-start | bytes 262144 | tf_op jit(solution)/shard_map/all_to_all | solution.py:37
  27.4 0.1 copy.33
  27.4 0.1 copy.34
  27.5 0.1 copy.37
  27.6 0.1 reshape.84
  27.7 0.6 gather_fusion
  28.4 0.1 reshape.83
  28.5 0.8 broadcast_select_fusion
  29.3 5.3 %all-to-all-done.2 = bf16[8,2,4096]{2,1,0:T(2,128)(2,1)S(1)} async-done(((bf16[8,2,4096]{2,1,0:T(2,128)(2,1)}), bf16[8,2,4096]{2,1,0:T(2,128)(2,1)S(1)}, u32[]{:S(2)}, u32[]{:S(2)}) %all-to-all-start.2) | async-done | bytes 131104 | tf_op jit(solution)/shard_map/all_to_all | solution.py:37
  34.6 3.4 %all-to-all-start.1 = ((bf16[8,2,4096]{2,1,0:T(2,128)(2,1)}), bf16[8,2,4096]{2,1,0:T(2,128)(2,1)S(1)}, u32[]{:S(2)}, u32[]{:S(2)}) async-start(bf16[8,2,4096]{2,1,0:T(2,128)(2,1)} %broadcast_select_fusion), calls=%async_computation.1 | async-start | bytes 262144 | tf_op jit(solution)/shard_map/all_to_all | solution.py:36
  38.0 0.0 all-reduce.2.cloned.1.call-start
  38.1 0.5 broadcast.107
  38.6 0.7 reduce.3
  39.3 0.1 eq.53
  39.3 0.1 reshape.81
  39.4 5.9 %all-to-all-done.1 = bf16[8,2,4096]{2,1,0:T(2,128)(2,1)S(1)} async-done(((bf16[8,2,4096]{2,1,0:T(2,128)(2,1)}), bf16[8,2,4096]{2,1,0:T(2,128)(2,1)S(1)}, u32[]{:S(2)}, u32[]{:S(2)}) %all-to-all-start.1) | async-done | bytes 131104 | tf_op jit(solution)/shard_map/all_to_all | solution.py:36
  45.3 0.1 reshape.78
  45.4 0.6 gather_fusion.1
  46.0 0.3 fusion.15
  46.3 0.3 fusion.5
  46.5 0.1 fusion
  46.7 2.1 %fusion.8 = f32[1024,256]{1,0:T(8,128)} fusion(bf16[4,8,8,128]{3,2,1,0:T(8,128)(2,1)S(1)} %bitcast.68, bf16[128,256]{1,0:T(8,128)(2,1)} %param.10, s32[]{:T(128)S(6)} %select_n.53), kind=kOutput, calls=%fused_computation.19 | convolution fusion | flops 16777216 | bytes 1130500 | tf_op jit(solution)/shard_map/dot_general | solution.py:55
  48.8 0.0 copy-start.4
  48.8 0.0 all-reduce.2.cloned.1.call-update
  48.8 34.0 %all-reduce.2.cloned.1.call-done = f32[1024,256]{1,0:T(8,128)} async-done(((f32[1024,256]{1,0:T(8,128)}), f32[1024,256]{1,0:T(8,128)}) %all-reduce.2.cloned.1.call-update) | async-done | bytes 1048592 | tf_op jit(solution)/shard_map/psum | solution.py:58
  82.8 0.0 copy-done.4
  82.8 1.8 %fusion.2 = f32[32,256]{1,0:T(8,128)S(1)} fusion(f32[1024,256]{1,0:T(8,128)} %all-reduce.2.cloned.1.call-done, bf16[1024,256]{1,0:T(8,128)(2,1)S(1)} %copy-done.4, bf16[4,8,8,128]{3,2,1,0:T(8,128)(2,1)S(1)} %bitcast.69), kind=kOutput, calls=%fused_computation.12 | convolution fusion | flops 19398656 | bytes 1671168 | tf_op jit(solution)/shard_map/dot_general | solution.py:64
  84.6 37.7 %psum.15 = f32[32,256]{1,0:T(8,128)} all-reduce(f32[32,256]{1,0:T(8,128)S(1)} %fusion.2), channel_id=1, replica_groups=mesh['row'=8,'col'=4] {'row'}, use_global_device_ids=true, to_apply=%region_5.6 | all-reduce | flops 8192 | bytes 65536 | tf_op jit(solution)/shard_map/psum | solution.py:65
  122.3 0.0 copy-done.1
  122.3 1.1 multiply_convert_fusion.1
  (10 shorter events, 0.1 us)
Async XLA Ops:
  7.2 11.9 %copy-start = (bf16[8,128,128]{2,1,0:T(8,128)(2,1)S(1)}, bf16[8,128,128]{2,1,0:T(8,128)(2,1)}, u32[]{:S(2)}) copy-start(bf16[8,128,128]{2,1,0:T(8,128)(2,1)} %param.7) | copy-start | bytes 786436
  7.9 0.7 copy-start.2
  10.2 7.4 %copy-start.3 = (s32[8,2]{0,1:T(2,128)S(1)}, s32[8,2]{0,1:T(2,128)}, u32[]{:S(2)}) copy-start(s32[8,2]{0,1:T(2,128)} %param.9) | copy-start | bytes 196
  10.2 13.8 %all-to-all-start = ((s32[8,1,2]{2,1,0:T(1,128)}), s32[8,1,2]{2,1,0:T(1,128)S(1)}, u32[]{:S(2)}, u32[]{:S(2)}) async-start(s32[8,1,2]{2,1,0:T(1,128)} %bitcast.7), calls=%async_computation | async-start | bytes 8192 | tf_op jit(solution)/shard_map/all_to_all | solution.py:34
  24.0 10.7 %all-to-all-start.2 = ((bf16[8,2,4096]{2,1,0:T(2,128)(2,1)}), bf16[8,2,4096]{2,1,0:T(2,128)(2,1)S(1)}, u32[]{:S(2)}, u32[]{:S(2)}) async-start(bf16[8,2,4096]{2,1,0:T(2,128)(2,1)} %reshape.80), calls=%async_computation.2 | async-start | bytes 262144 | tf_op jit(solution)/shard_map/all_to_all | solution.py:37
  34.6 10.7 %all-to-all-start.1 = ((bf16[8,2,4096]{2,1,0:T(2,128)(2,1)}), bf16[8,2,4096]{2,1,0:T(2,128)(2,1)S(1)}, u32[]{:S(2)}, u32[]{:S(2)}) async-start(bf16[8,2,4096]{2,1,0:T(2,128)(2,1)} %broadcast_select_fusion), calls=%async_computation.1 | async-start | bytes 262144 | tf_op jit(solution)/shard_map/all_to_all | solution.py:36
  38.0 44.8 %all-reduce.2.cloned.1.call-start = ((), (), s32[]{:S(2)}) async-start(), calls=%async_computation.3 | async-start | bytes 2097152 | tf_op jit(solution)/shard_map/psum | solution.py:58
  48.8 34.0 %copy-start.4 = (bf16[1024,256]{1,0:T(8,128)(2,1)S(1)}, bf16[1024,256]{1,0:T(8,128)(2,1)}, u32[]{:S(2)}) copy-start(bf16[1024,256]{1,0:T(8,128)(2,1)} %param.11) | copy-start | bytes 1572868
  82.8 39.5 %copy-start.1 = (f32[1024,256]{1,0:T(8,128)S(1)}, f32[1024,256]{1,0:T(8,128)}, u32[]{:S(2)}) copy-start(f32[1024,256]{1,0:T(8,128)} %all-reduce.2.cloned.1.call-done) | copy-start | bytes 3145732
Sparse Core Ops, SparseCore 0:
  48.9 33.8 all-reduce.1
where the time goes:
time: 131 us; the launch traced here: 130 us
  waiting for transfers between devices  48.4 us (37%)
  blocking collectives  37.7 us (29%)
  starting transfers between devices  14.2 us (11%)
  between operations  14.2 us (11%)
  local copies, waits for them, and re-layouts  7.28 us (6%)
  matrix products  4.85 us (4%)
  other arithmetic  3.66 us (3%)
    psum x1, blocking collectives, body(): grad_w = lax.psum(grad_part, 'row')  37.7 us
    psum x1, waiting for transfers between devices, body(): y_full = lax.psum(partial_y, 'col')  34 us
    all_to_all x1, starting transfers between devices, body(): lax.all_to_all(requests, 'row', split_axis=0, concat_axis=0, tiled=True)  7.41 us
    all_to_all x1, waiting for transfers between devices, body(): lax.all_to_all(picked, 'row', split_axis=0, concat_axis=0, tiled=True)  5.9 us
    all_to_all x1, waiting for transfers between devices, body(): lax.all_to_all(outgoing, 'row', split_axis=0, concat_axis=0, tiled=True)  5.33 us
    all_to_all x1, starting transfers between devices, body(): lax.all_to_all(picked, 'row', split_axis=0, concat_axis=0, tiled=True)  3.37 us
    all_to_all x1, starting transfers between devices, body(): lax.all_to_all(outgoing, 'row', split_axis=0, concat_axis=0, tiled=True)  3.37 us
    all_to_all x1, waiting for transfers between devices, body(): lax.all_to_all(requests, 'row', split_axis=0, concat_axis=0, tiled=True)  3.14 us
  transfers between devices with their start and end apart: 4, of which 4 were waited for; matrix products, arithmetic and copies ran while one was open for 5% of the time, Pallas kernels for 0%

commit v1 on v0

--- a/solution.py
+++ b/solution.py
@@ -2,6 +2,18 @@
 import jax.numpy as jnp
 from jax import lax
 from jax.sharding import PartitionSpec as P
+
+
+def split_up(x, dim, size):
+    dims = x.shape
+    blocks = x.reshape(*dims[:dim], size, dims[dim] // size, *dims[dim + 1 :])
+    return jnp.moveaxis(blocks, dim, 0)
+
+
+def laid_out(blocks, dim):
+    blocks = jnp.moveaxis(blocks, 0, dim)
+    lengths = blocks.shape
+    return blocks.reshape(*lengths[:dim], lengths[dim] * lengths[dim + 1], *lengths[dim + 2 :])
 
 
 def body(x_t, tiles, tile_owner, tile_local, weight, cotangent):
@@ -31,7 +43,14 @@
         .set(mirror_terms.reshape(n_tiles, feat_q * tile_dim))
         .reshape(n_row, capacity, feat_q * tile_dim)
     )
-    block_ids = lax.all_to_all(requests, "row", split_axis=0, concat_axis=0, tiled=True)
+    peers, index = (lax.axis_size("row"), lax.axis_index("row"))
+    pieces = split_up(requests, 0, peers)
+    outs = [pieces[index]]
+    for step in range(1, peers):
+        sent = pieces[index ^ step]
+        outs.append(lax.ppermute(sent, "row", [(i, i ^ step) for i in range(peers)]))
+    pieces = jnp.stack(outs)[index ^ jnp.arange(peers)]
+    block_ids = laid_out(pieces, 0)
     picked = jnp.take(flat_blocks, block_ids, axis=0)
     fetched = lax.all_to_all(picked, "row", split_axis=0, concat_axis=0, tiled=True)
     incoming = lax.all_to_all(outgoing, "row", split_axis=0, concat_axis=0, tiled=True)

time: 131 us -> 133 us (1.015)
  starting transfers between devices: 14.2 us -> 23.7 us
  waiting for transfers between devices: 48.4 us -> 42.8 us
  other arithmetic: 3.66 us -> 2.25 us
    ppermute x0 -> x7, starting transfers between devices: none -> 14.9 us  [body(): lax.ppermute(sent, 'row', [(i, i ^ step) for i in range(peers)])]
    all_to_all x1 -> x0, starting transfers between devices: 7.41 us -> none  [body(): lax.all_to_all(requests, 'row', split_axis=0, concat_axis=0, tiled=True)]
    all_to_all x1, waiting for transfers between devices: 5.33 us -> 0.01 us  [body(): lax.all_to_all(outgoing, 'row', split_axis=0, concat_axis=0, tiled=True)]
    all_to_all x1 -> x0, waiting for transfers between devices: 3.14 us -> none  [body(): lax.all_to_all(requests, 'row', split_axis=0, concat_axis=0, tiled=True)]
    ppermute x0 -> x7, waiting for transfers between devices: none -> 1.62 us  [body(): lax.ppermute(sent, 'row', [(i, i ^ step) for i in range(peers)])]
  transfers between devices with their start and end apart: 4 -> 10, of which waited for: 4 -> 3; matrix products, arithmetic and copies ran while one was open for 5% -> 4% of each run, Pallas kernels for 0% -> 0%
where the time goes in v1:
time: 133 us; the launch traced here: 132 us
  waiting for transfers between devices  42.8 us (32%)
  blocking collectives  37.7 us (28%)
  starting transfers between devices  23.7 us (18%)
  between operations  14.3 us (11%)
  local copies, waits for them, and re-layouts  6.77 us (5%)
  matrix products  4.84 us (4%)
  other arithmetic  2.25 us (2%)
    psum x1, blocking collectives, body(): grad_w = lax.psum(grad_part, 'row')  37.7 us
    psum x1, waiting for transfers between devices, body(): y_full = lax.psum(partial_y, 'col')  34 us
    ppermute x7, starting transfers between devices, body(): lax.ppermute(sent, 'row', [(i, i ^ step) for i in range(peers)])  14.9 us
    all_to_all x1, waiting for transfers between devices, body(): lax.all_to_all(picked, 'row', split_axis=0, concat_axis=0, tiled=True)  7.14 us
    all_to_all x1, starting transfers between devices, body(): lax.all_to_all(picked, 'row', split_axis=0, concat_axis=0, tiled=True)  4.54 us
    all_to_all x1, starting transfers between devices, body(): lax.all_to_all(outgoing, 'row', split_axis=0, concat_axis=0, tiled=True)  4.2 us
  transfers between devices with their start and end apart: 10, of which 3 were waited for; matrix products, arithmetic and copies ran while one was open for 4% of the time, Pallas kernels for 0%

profile of v1, /device:TPU:0, one launch (start us, length us, event | category | flops | bytes accessed | tf_op | source)
XLA Modules:
  0.0 132.3 jit_solution(15235029811024995240)
XLA Ops:
  7.2 0.7 copy-done.4
  7.9 0.1 fusion.24
  8.0 0.2 select_reduce_fusion
  8.2 0.6 scatter_custom_fusion
  8.8 0.1 reshape_reshape.3
  8.9 6.1 %collective-permute-start.6 = (s32[1,2]{1,0:T(1,128)S(1)}, s32[1,2]{1,0:T(1,128)S(1)}, u32[]{:S(2)}, u32[]{:S(2)}) collective-permute-start(s32[1,2]{1,0:T(1,128)S(1)} %get-tuple-element.6), channel_id=1, source_target_pairs={{0,28},{4,24},{8,20},{12,16},{16,12},{20,8},{24,4},{28,0},{1,29},{... | collective-permute-start | bytes 32 | tf_op jit(solution)/shard_map/ppermute | solution.py:51
  15.0 0.2 collective-permute-start.5
  15.2 0.7 collective-permute-start.4
  15.9 2.0 %collective-permute-start.3 = (s32[1,2]{1,0:T(1,128)S(1)}, s32[1,2]{1,0:T(1,128)S(1)}, u32[]{:S(2)}, u32[]{:S(2)}) collective-permute-start(s32[1,2]{1,0:T(1,128)S(1)} %get-tuple-element.9), channel_id=1, source_target_pairs={{0,16},{4,20},{8,24},{12,28},{16,0},{20,4},{24,8},{28,12},{1,17},{... | collective-permute-start | bytes 32 | tf_op jit(solution)/shard_map/ppermute | solution.py:51
  18.0 2.3 %collective-permute-start.2 = (s32[1,2]{1,0:T(1,128)S(1)}, s32[1,2]{1,0:T(1,128)S(1)}, u32[]{:S(2)}, u32[]{:S(2)}) collective-permute-start(s32[1,2]{1,0:T(1,128)S(1)} %get-tuple-element.10), channel_id=1, source_target_pairs={{0,12},{4,8},{8,4},{12,0},{16,28},{20,24},{24,20},{28,16},{1,13},{... | collective-permute-start | bytes 32 | tf_op jit(solution)/shard_map/ppermute | solution.py:51
  20.3 0.6 gather_fusion.3
  20.9 0.2 fusion.1
  21.1 0.8 scatter_custom_fusion.1
  21.9 0.8 reshape.98
  22.7 4.2 %all-to-all-start.1 = ((bf16[8,2,4096]{2,1,0:T(2,128)(2,1)}), bf16[8,2,4096]{2,1,0:T(2,128)(2,1)S(1)}, u32[]{:S(2)}, u32[]{:S(2)}) async-start(bf16[8,2,4096]{2,1,0:T(2,128)(2,1)} %reshape.98), calls=%async_computation.1 | async-start | bytes 262144 | tf_op jit(solution)/shard_map/all_to_all | solution.py:56
  26.9 0.1 copy.59
  27.0 2.1 %collective-permute-start.1 = (s32[1,2]{1,0:T(1,128)S(1)}, s32[1,2]{1,0:T(1,128)S(1)}, u32[]{:S(2)}, u32[]{:S(2)}) collective-permute-start(s32[1,2]{1,0:T(1,128)S(1)} %get-tuple-element.11), channel_id=1, source_target_pairs={{0,8},{4,12},{8,0},{12,4},{16,24},{20,28},{24,16},{28,20},{1,9},{5... | collective-permute-start | bytes 32 | tf_op jit(solution)/shard_map/ppermute | solution.py:51
  29.1 0.1 copy.66
  29.2 1.5 %collective-permute-start = (s32[1,2]{1,0:T(1,128)S(1)}, s32[1,2]{1,0:T(1,128)S(1)}, u32[]{:S(2)}, u32[]{:S(2)}) collective-permute-start(s32[1,2]{1,0:T(1,128)S(1)} %get-tuple-element.12), channel_id=1, source_target_pairs={{0,4},{4,0},{8,12},{12,8},{16,20},{20,16},{24,28},{28,24},{1,5},{5... | collective-permute-start | bytes 32 | tf_op jit(solution)/shard_map/ppermute | solution.py:51
  30.7 0.1 copy.65
  30.8 0.1 copy.64
  30.8 0.1 copy.63
  30.9 0.1 copy.62
  31.0 0.1 copy.61
  31.1 1.6 %collective-permute-done = s32[1,2]{1,0:T(1,128)S(1)} collective-permute-done((s32[1,2]{1,0:T(1,128)S(1)}, s32[1,2]{1,0:T(1,128)S(1)}, u32[]{:S(2)}, u32[]{:S(2)}) %collective-permute-start) | collective-permute-done | bytes 40 | tf_op jit(solution)/shard_map/ppermute | solution.py:51
  32.7 0.1 copy.60
  32.8 0.1 stack.31
  32.9 0.1 copy.67
  33.0 0.6 gather_fusion
  33.6 0.1 copy.69
  33.7 0.1 copy.70
  33.8 0.1 reshape.112
  33.8 0.6 gather_fusion.1
  34.5 0.1 reshape.111
  34.6 0.8 broadcast_select_fusion
  35.4 4.5 %all-to-all-start = ((bf16[8,2,4096]{2,1,0:T(2,128)(2,1)}), bf16[8,2,4096]{2,1,0:T(2,128)(2,1)S(1)}, u32[]{:S(2)}, u32[]{:S(2)}) async-start(bf16[8,2,4096]{2,1,0:T(2,128)(2,1)} %broadcast_select_fusion), calls=%async_computation | async-start | bytes 262144 | tf_op jit(solution)/shard_map/all_to_all | solution.py:55
  40.0 0.1 eq.53
  40.2 7.1 %all-to-all-done = bf16[8,2,4096]{2,1,0:T(2,128)(2,1)S(1)} async-done(((bf16[8,2,4096]{2,1,0:T(2,128)(2,1)}), bf16[8,2,4096]{2,1,0:T(2,128)(2,1)S(1)}, u32[]{:S(2)}, u32[]{:S(2)}) %all-to-all-start) | async-done | bytes 131104 | tf_op jit(solution)/shard_map/all_to_all | solution.py:55
  47.3 0.1 reshape.96
  47.4 0.6 gather_fusion.2
  48.0 0.3 fusion.15
  48.3 0.3 fusion.5
  48.6 0.1 fusion
  48.7 2.1 %fusion.8 = f32[1024,256]{1,0:T(8,128)} fusion(bf16[4,8,8,128]{3,2,1,0:T(8,128)(2,1)S(1)} %bitcast.89, bf16[128,256]{1,0:T(8,128)(2,1)} %param.10, s32[]{:T(128)S(6)} %select_n.96), kind=kOutput, calls=%fused_computation.20 | convolution fusion | flops 16777216 | bytes 1130500 | tf_op jit(solution)/shard_map/dot_general | solution.py:74
  50.8 34.0 %all-reduce.2.cloned.1.call-done = f32[1024,256]{1,0:T(8,128)} async-done(((f32[1024,256]{1,0:T(8,128)}), f32[1024,256]{1,0:T(8,128)}) %all-reduce.2.cloned.1.call-update) | async-done | bytes 1048592 | tf_op jit(solution)/shard_map/psum | solution.py:77
  84.8 1.8 %fusion.2 = f32[32,256]{1,0:T(8,128)S(1)} fusion(f32[1024,256]{1,0:T(8,128)} %all-reduce.2.cloned.1.call-done, bf16[1024,256]{1,0:T(8,128)(2,1)S(1)} %copy-done.5, bf16[4,8,8,128]{3,2,1,0:T(8,128)(2,1)S(1)} %bitcast.90), kind=kOutput, calls=%fused_computation.13 | convolution fusion | flops 19398656 | bytes 1671168 | tf_op jit(solution)/shard_map/dot_general | solution.py:83
  86.7 37.7 %psum.15 = f32[32,256]{1,0:T(8,128)} all-reduce(f32[32,256]{1,0:T(8,128)S(1)} %fusion.2), channel_id=1, replica_groups=mesh['row'=8,'col'=4] {'row'}, use_global_device_ids=true, to_apply=%region_5.6 | all-reduce | flops 8192 | bytes 65536 | tf_op jit(solution)/shard_map/psum | solution.py:84
  124.3 1.1 multiply_convert_fusion.1
  (34 shorter events, 0.3 us)
Async XLA Ops:
  7.2 13.7 %copy-start = (bf16[8,128,128]{2,1,0:T(8,128)(2,1)S(1)}, bf16[8,128,128]{2,1,0:T(8,128)(2,1)}, u32[]{:S(2)}) copy-start(bf16[8,128,128]{2,1,0:T(8,128)(2,1)} %param.7) | copy-start | bytes 786436
  7.2 0.7 copy-start.4
  7.2 0.7 copy-start.3
  7.2 13.1 %copy-start.2 = (bf16[32,1024]{1,0:T(8,128)(2,1)S(1)}, bf16[32,1024]{1,0:T(8,128)(2,1)}, u32[]{:S(2)}) copy-start(bf16[32,1024]{1,0:T(8,128)(2,1)} %param.6) | copy-start | bytes 196612
  8.9 18.1 %collective-permute-start.6 = (s32[1,2]{1,0:T(1,128)S(1)}, s32[1,2]{1,0:T(1,128)S(1)}, u32[]{:S(2)}, u32[]{:S(2)}) collective-permute-start(s32[1,2]{1,0:T(1,128)S(1)} %get-tuple-element.6), channel_id=1, source_target_pairs={{0,28},{4,24},{8,20},{12,16},{16,12},{20,8},{24,4},{28,0},{1,29},{... | collective-permute-start | bytes 32 | tf_op jit(solution)/shard_map/ppermute | solution.py:51
  15.0 14.2 %collective-permute-start.5 = (s32[1,2]{1,0:T(1,128)S(1)}, s32[1,2]{1,0:T(1,128)S(1)}, u32[]{:S(2)}, u32[]{:S(2)}) collective-permute-start(s32[1,2]{1,0:T(1,128)S(1)} %get-tuple-element.7), channel_id=1, source_target_pairs={{0,24},{4,28},{8,16},{12,20},{16,8},{20,12},{24,0},{28,4},{1,25},{... | collective-permute-start | bytes 32 | tf_op jit(solution)/shard_map/ppermute | solution.py:51
  15.2 15.5 %collective-permute-start.4 = (s32[1,2]{1,0:T(1,128)S(1)}, s32[1,2]{1,0:T(1,128)S(1)}, u32[]{:S(2)}, u32[]{:S(2)}) collective-permute-start(s32[1,2]{1,0:T(1,128)S(1)} %get-tuple-element.8), channel_id=1, source_target_pairs={{0,20},{4,16},{8,28},{12,24},{16,4},{20,0},{24,12},{28,8},{1,21},{... | collective-permute-start | bytes 32 | tf_op jit(solution)/shard_map/ppermute | solution.py:51
  15.9 14.9 %collective-permute-start.3 = (s32[1,2]{1,0:T(1,128)S(1)}, s32[1,2]{1,0:T(1,128)S(1)}, u32[]{:S(2)}, u32[]{:S(2)}) collective-permute-start(s32[1,2]{1,0:T(1,128)S(1)} %get-tuple-element.9), channel_id=1, source_target_pairs={{0,16},{4,20},{8,24},{12,28},{16,0},{20,4},{24,8},{28,12},{1,17},{... | collective-permute-start | bytes 32 | tf_op jit(solution)/shard_map/ppermute | solution.py:51
  18.0 12.9 %collective-permute-start.2 = (s32[1,2]{1,0:T(1,128)S(1)}, s32[1,2]{1,0:T(1,128)S(1)}, u32[]{:S(2)}, u32[]{:S(2)}) collective-permute-start(s32[1,2]{1,0:T(1,128)S(1)} %get-tuple-element.10), channel_id=1, source_target_pairs={{0,12},{4,8},{8,4},{12,0},{16,28},{20,24},{24,20},{28,16},{1,13},{... | collective-permute-start | bytes 32 | tf_op jit(solution)/shard_map/ppermute | solution.py:51
  22.7 12.8 %all-to-all-start.1 = ((bf16[8,2,4096]{2,1,0:T(2,128)(2,1)}), bf16[8,2,4096]{2,1,0:T(2,128)(2,1)S(1)}, u32[]{:S(2)}, u32[]{:S(2)}) async-start(bf16[8,2,4096]{2,1,0:T(2,128)(2,1)} %reshape.98), calls=%async_computation.1 | async-start | bytes 262144 | tf_op jit(solution)/shard_map/all_to_all | solution.py:56
  27.0 4.0 %collective-permute-start.1 = (s32[1,2]{1,0:T(1,128)S(1)}, s32[1,2]{1,0:T(1,128)S(1)}, u32[]{:S(2)}, u32[]{:S(2)}) collective-permute-start(s32[1,2]{1,0:T(1,128)S(1)} %get-tuple-element.11), channel_id=1, source_target_pairs={{0,8},{4,12},{8,0},{12,4},{16,24},{20,28},{24,16},{28,20},{1,9},{5... | collective-permute-start | bytes 32 | tf_op jit(solution)/shard_map/ppermute | solution.py:51
  29.2 3.5 %collective-permute-start = (s32[1,2]{1,0:T(1,128)S(1)}, s32[1,2]{1,0:T(1,128)S(1)}, u32[]{:S(2)}, u32[]{:S(2)}) collective-permute-start(s32[1,2]{1,0:T(1,128)S(1)} %get-tuple-element.12), channel_id=1, source_target_pairs={{0,4},{4,0},{8,12},{12,8},{16,20},{20,16},{24,28},{28,24},{1,5},{5... | collective-permute-start | bytes 32 | tf_op jit(solution)/shard_map/ppermute | solution.py:51
  35.4 11.9 %all-to-all-start = ((bf16[8,2,4096]{2,1,0:T(2,128)(2,1)}), bf16[8,2,4096]{2,1,0:T(2,128)(2,1)S(1)}, u32[]{:S(2)}, u32[]{:S(2)}) async-start(bf16[8,2,4096]{2,1,0:T(2,128)(2,1)} %broadcast_select_fusion), calls=%async_computation | async-start | bytes 262144 | tf_op jit(solution)/shard_map/all_to_all | solution.py:55
  40.0 44.8 %all-reduce.2.cloned.1.call-start = ((), (), s32[]{:S(2)}) async-start(), calls=%async_computation.2 | async-start | bytes 2097152 | tf_op jit(solution)/shard_map/psum | solution.py:77
  50.8 34.0 %copy-start.5 = (bf16[1024,256]{1,0:T(8,128)(2,1)S(1)}, bf16[1024,256]{1,0:T(8,128)(2,1)}, u32[]{:S(2)}) copy-start(bf16[1024,256]{1,0:T(8,128)(2,1)} %param.11) | copy-start | bytes 1572868
  84.8 39.5 %copy-start.1 = (f32[1024,256]{1,0:T(8,128)S(1)}, f32[1024,256]{1,0:T(8,128)}, u32[]{:S(2)}) copy-start(f32[1024,256]{1,0:T(8,128)} %all-reduce.2.cloned.1.call-done) | copy-start | bytes 3145732
Sparse Core Ops, SparseCore 0:
  50.9 33.8 all-reduce.1
